TPU v7x, 512 devices: a whole 4x4x16 slice. The times are simulated.
512 devices in a mesh: seq: 8 (over x, core), tp: 16 (over z), req: 4 (over y).
Axes of the slice: x: 4, y: 4, z: 16, core: 2. Of those that a mesh axis runs over, the one named last changes fastest.
Arguments:
- tokens: bfloat16 [32768, 1792], P(('req', 'seq'), 'tp'), parts along dimension 0, may hold values from -6 to 6
- w_in: bfloat16 [1792, 4096], P(None, 'tp'), may hold values from -0.125 to 0.125
- conv_w: float32 [3, 1792], P(None, 'tp'), may hold values from -3 to 3
- head_gain: float32 [1792], P('tp'), may hold values from 0.1 to 1.9
- w_out: bfloat16 [1792, 1792], P('tp'), may hold values from -0.125 to 0.125
- prompt_lens: int32 [16], P('req'), parts along dimension 0, may hold values from 1 to 4096, 8192 in all
- req_group: int32 [128], P('req'), parts along dimension 0, may hold values from 0 to 3, as said below
- row_request: int32 [128], P('req'), parts along dimension 0, may hold values from 0 to 31, each once
Outputs:
- mixed: bfloat16 [32768, 1792], P(('req', 'seq'), 'tp'), parts along dimension 0
- req_state: float32 [128, 16, 273, 112], P(('req', 'seq'), 'tp'), parts along dimension 0
- req_norm: float32 [128, 16, 273], P(('req', 'seq'), 'tp'), parts along dimension 0
- req_edge: bfloat16 [128, 2, 1792], P(('req', 'seq'), None, 'tp'), parts along dimension 0
There are 4 independent parts, one for each index of `req`. A program takes and returns all parts, laid end to end along the dimension named above; an argument that names none is the same for every part. Nothing has to cross between parts.
Inputs may be any that keep to these rules, and one draw needn't show every extreme that they name: `prompt_lens`: the lengths sum to 8192, and the largest is half of 8192. `req_group`: every one of the 4 prompts is shared by at least one request. `row_request`: each request appears once; rows i * 4 to (i + 1) * 4 - 1 lie on index i of seq.
All inputs are finite; a program needn't handle non-finite values.
Results may differ from a plain program's by a relative error of at most 0.019.
Values may be sent and summed in bfloat16 or wider, within the bound.
No kernel may reach another device: no remote copies, remote signals or barrier semaphores. Data moves between devices by JAX's collectives and lax.ppermute only.
A program may use at most 64 MiB of HBM per device.

v0:
```python
import jax
import jax.numpy as jnp
from jax import lax
from jax.sharding import PartitionSpec as P

FEAT = 16
HD = 112
KW = 3
PROMPTS = 4
SLOTS = 4
EPS = 1e-05
HIGH = lax.Precision.HIGHEST


def passed_along(shard, axis, by):
    size = lax.axis_size(axis)
    pairs = [(i, i + by) for i in range(size) if 0 <= i + by < size]
    return lax.ppermute(shard, axis, pairs)


def psum_doubling(parts, axis):
    size = lax.axis_size(axis)
    total = [p.astype(jnp.float32) for p in parts]
    step = 1
    while step < size:
        pairs = [(i, i ^ step) for i in range(size)]
        got = lax.ppermute(tuple((t.astype(jnp.bfloat16) for t in total)), axis, pairs)
        total = [t + g.astype(jnp.float32) for t, g in zip(total, got)]
        step *= 2
    return total


def tail_prefix(tail, tail_seg, axis):
    size, here = (lax.axis_size(axis), lax.axis_index(axis))
    seg_before = tail_seg[jnp.maximum(here - 1, 0)]
    group = tail.astype(jnp.float32)
    before = jnp.zeros_like(group)
    step = 1
    while step < size:
        pairs = [(i, i ^ step) for i in range(size)]
        got = lax.ppermute(group.astype(jnp.bfloat16), axis, pairs).astype(jnp.float32)
        other = here ^ step
        my_end = here | step - 1
        other_end = other | step - 1
        same = (tail_seg[my_end] == tail_seg[other_end]).astype(jnp.float32)
        earlier = other < here
        take = (earlier & (tail_seg[other_end] == seg_before)).astype(jnp.float32)
        before = before + take * got
        group = jnp.where(earlier, group + same * got, got + same * group)
        step *= 2
    return before


def taylor_map(values):
    size = values.shape[-1]
    ones = jnp.ones(values.shape[:-1] + (1,), jnp.float32)
    pairs = (values[..., :, None] * values[..., None, :]).reshape(
        values.shape[:-1] + (size * size,)
    )
    return jnp.concatenate([ones, values, pairs * 0.5**0.5], axis=-1)


def segment_ids(positions, ends):
    return jnp.sum((positions[:, None] >= ends[None, :]).astype(jnp.int32), axis=1)


def local(tokens, w_in, conv_w, head_gain, w_out, prompt_lens, req_group, row_request):
    tok_rows = tokens.shape[0]
    width = 2 * FEAT + 2 * HD
    local_heads = w_in.shape[1] // width
    local_cols = local_heads * HD
    seq_pos = lax.axis_index("seq")
    first_row = seq_pos * tok_rows
    ends = jnp.cumsum(prompt_lens)
    starts = ends - prompt_lens
    positions = first_row + jnp.arange(tok_rows, dtype=jnp.int32)
    seg = segment_ids(positions, ends)
    half = tok_rows // 2
    proj_halves = [
        jnp.dot(
            lax.all_gather(part, "tp", axis=1, tiled=True), w_in, preferred_element_type=jnp.float32
        )
        .astype(jnp.bfloat16)
        .reshape(half, local_heads, width)
        for part in (tokens[:half], tokens[half:])
    ]
    proj = jnp.concatenate(proj_halves, axis=0)
    gate_pre = proj[:, :, 2 * FEAT + HD :].reshape(tok_rows, local_cols)
    rim = passed_along(gate_pre[tok_rows - (KW - 1) :], "seq", 1)
    extended = jnp.concatenate([rim, gate_pre], 0)
    ext_pos = first_row - (KW - 1) + jnp.arange(tok_rows + KW - 1, dtype=jnp.int32)
    ext_seg = segment_ids(ext_pos, ends)
    gate = jnp.zeros((tok_rows, local_cols), jnp.float32)
    for tap in range(KW):
        low = KW - 1 - tap
        same = (ext_seg[low : low + tok_rows] == seg).astype(jnp.float32)
        gate = (
            gate
            + conv_w[tap][None, :]
            * extended[low : low + tok_rows].astype(jnp.float32)
            * same[:, None]
        )
    qs_b = proj[:, :, :FEAT] * jnp.bfloat16(FEAT ** (-0.25))
    ks_b = proj[:, :, FEAT : 2 * FEAT] * jnp.bfloat16(FEAT ** (-0.25))
    qs = qs_b.astype(jnp.float32)
    ks = ks_b.astype(jnp.float32)
    values = proj[:, :, 2 * FEAT : 2 * FEAT + HD]
    values_f = values.astype(jnp.float32)
    numer_halves = []
    for lo, hi in ((0, half), (half, tok_rows)):
        dots = jnp.einsum(
            "thf,shf->hts", qs_b[lo:hi], ks_b[:hi], preferred_element_type=jnp.float32
        )
        visible = (positions[None, :hi] <= positions[lo:hi, None]) & (
            seg[lo:hi, None] == seg[None, :hi]
        )
        weights = jnp.where(visible[None], 1.0 + dots + 0.5 * dots * dots, 0.0)
        numer_halves.append(
            jnp.einsum(
                "hts,shd->thd",
                weights.astype(jnp.bfloat16),
                values[:hi],
                preferred_element_type=jnp.float32,
            )
        )
    numer = jnp.concatenate(numer_halves, axis=0)
    phi_q = taylor_map(qs)
    phi_k = taylor_map(ks)
    fmap = phi_k.shape[-1]
    prompt_index = jnp.arange(PROMPTS, dtype=jnp.int32)
    onehot = (seg[:, None] == prompt_index[None, :]).astype(jnp.float32)
    keyed = (onehot[:, :, None, None] * phi_k[:, None, :, :]).reshape(
        tok_rows, PROMPTS * local_heads * fmap
    )
    contrib_state = lax.dot_general(
        keyed.reshape(tok_rows, PROMPTS, local_heads, fmap),
        values_f,
        (((0,), (0,)), ((2,), (1,))),
        precision=HIGH,
    )
    contrib_norm = jnp.einsum("tg,thf->ghf", onehot, phi_k, precision=HIGH)
    offsets = jnp.arange(KW - 1, dtype=jnp.int32)
    edge_rows = ends[:, None] - (KW - 1) + offsets[None, :]
    edge_valid = edge_rows >= starts[:, None]
    match = ((positions[:, None, None] == edge_rows[None]) & edge_valid[None]).astype(jnp.bfloat16)
    contrib_edge = jnp.einsum("tgj,tc->gjc", match, gate_pre, preferred_element_type=jnp.float32)
    block_ends = (jnp.arange(lax.axis_size("seq"), dtype=jnp.int32) + 1) * tok_rows - 1
    tail_seg = segment_ids(block_ends, ends)
    seg_last = tail_seg[seq_pos]
    in_tail = (seg == seg_last).astype(jnp.float32)
    tail_state = sum(
        (
            jnp.einsum(
                "thf,thd->hfd",
                taylor_map(ks[lo:hi]) * in_tail[lo:hi, None, None],
                values_f[lo:hi],
                precision=HIGH,
            )
            for lo, hi in ((0, half), (half, tok_rows))
        )
    )
    seg_before = jnp.sum((first_row - 1 >= ends).astype(jnp.int32))
    tails = lax.all_gather(tail_state.astype(jnp.bfloat16), "seq").astype(jnp.float32)
    block_index = jnp.arange(lax.axis_size("seq"), dtype=jnp.int32)
    chained = ((block_index < seq_pos) & (tail_seg == seg_before)).astype(jnp.float32)
    carry_state = jnp.sum(chained.reshape((-1,) + (1,) * (tails.ndim - 1)) * tails, axis=0)
    carried = ((seg == seg_before) & (first_row > 0)).astype(jnp.float32)
    attended = (
        numer
        + jnp.einsum("thf,hfd->thd", phi_q, carry_state, precision=HIGH) * carried[:, None, None]
    )
    inv_rms = lax.rsqrt(jnp.mean(attended * attended, axis=2, keepdims=True) + EPS)
    gain = head_gain.reshape(local_heads, HD)
    hidden = (
        attended * inv_rms * gain[None] * jax.nn.silu(gate.reshape(tok_rows, local_heads, HD))
    ).astype(jnp.bfloat16)
    hidden = hidden.reshape(tok_rows, local_cols)
    product = jnp.einsum(
        "tk,kgc->gtc",
        hidden,
        w_out.reshape(local_cols, lax.axis_size("tp"), -1),
        preferred_element_type=jnp.bfloat16,
    )
    summed = lax.psum_scatter(product, "tp", scatter_dimension=0, tiled=True)
    mixed = summed.reshape(tok_rows, -1)
    all_state, all_norm, all_edge = psum_doubling(
        (contrib_state, contrib_norm, contrib_edge), "seq"
    )
    scale = lax.rsqrt(prompt_lens.astype(jnp.float32))
    my_requests = lax.dynamic_slice_in_dim(row_request, seq_pos * SLOTS, SLOTS)
    my_groups = jnp.take(req_group, my_requests)
    my_scale = jnp.take(scale, my_groups)
    req_state = (
        jnp.take(all_state, my_groups, axis=1).transpose(1, 0, 2, 3) * my_scale[:, None, None, None]
    )
    req_norm = jnp.take(all_norm, my_groups, axis=0) * my_scale[:, None, None]
    req_edge = jnp.take(all_edge, my_groups, axis=0).astype(jnp.bfloat16)
    return (mixed, req_state, req_norm, req_edge)


def solution(mesh):
    in_specs = (
        P(("req", "seq"), "tp"),
        P(None, "tp"),
        P(None, "tp"),
        P("tp"),
        P("tp", None),
        P("req"),
        P("req"),
        P("req"),
    )
    out_specs = (
        P(("req", "seq"), "tp"),
        P(("req", "seq"), "tp", None, None),
        P(("req", "seq"), "tp", None),
        P(("req", "seq"), None, "tp"),
    )
    return jax.shard_map(local, mesh=mesh, in_specs=in_specs, out_specs=out_specs, check_vma=False)
```

profile of v0, /device:TPU:4, one launch (start us, length us, event | category | flops | bytes accessed | tf_op | source)
XLA Modules:
  0.0 269.2 jit_solution(1293546007089729475)
XLA Ops:
  7.2 1.7 fusion.108
  9.0 0.7 all-gather.5.cloned.1.call-update
  9.8 0.8 reduce-window.7
  10.7 0.7 dynamic_slice.6
  11.6 1.9 bitcast_subtract_fusion
  13.5 1.2 and_convert_fusion.1
  14.7 1.4 slice_bitcast_fusion.21
  16.1 0.6 fusion.109
  16.6 0.6 fusion.110
  17.2 2.0 fusion.84
  19.2 68.1 %all-gather.7.cloned.1.call-done = bf16[512,1792]{0,1:T(8,128)(2,1)} async-done(((bf16[512,112]{0,1:T(8,128)(2,1)}), bf16[512,1792]{0,1:T(8,128)(2,1)}) %all-gather.7.cloned.1.call-update) | async-done | bytes 1835024 | tf_op jit(solution)/shard_map/all_gather | solution.py:81
  87.3 2.2 fusion.12
  89.5 0.7 slice_bitcast_fusion.9
  90.2 1.9 collective-permute-start
  92.1 66.9 %all-gather.5.cloned.1.call-done = bf16[512,1792]{0,1:T(8,128)(2,1)} async-done(((bf16[512,112]{0,1:T(8,128)(2,1)}), bf16[512,1792]{0,1:T(8,128)(2,1)}) %all-gather.5.cloned.1.call-update) | async-done | bytes 1835024 | tf_op jit(solution)/shard_map/all_gather | solution.py:81
  159.0 2.2 fusion.11
  161.6 0.5 fusion.32
  162.1 0.5 fusion.19
  162.6 12.0 %all-gather.1 = bf16[8,273,112]{2,1,0:T(8,128)(2,1)S(1)} all-gather(bf16[1,273,112]{2,1,0:T(8,128)(2,1)S(1)} %fusion.19), channel_id=2, replica_groups=mesh['seq'=8,'tp'=16,'req'=4] {'seq'}, dimensions={0}, use_global_device_ids=true | all-gather | bytes 550368 | tf_op jit(solution)/shard_map/all_gather | solution.py:163
  174.5 1.7 fusion.13
  176.2 2.1 convolution_bitcast_fusion.1
  178.4 1.0 fusion.17
  179.3 2.2 multiply_reduce_fusion
  181.6 4.0 %fusion.60 = bf16[1024,1792]{0,1} fusion(bf16[112,1792]{1,0:T(8,128)(2,1)S(1)} %copy-done.2, bf16[1024,112]{0,1:T(8,128)(2,1)S(1)} %fusion.92, f32[1024,1,112]{0,2,1:T(8,128)S(1)} %get-tuple-element.52, bf16[2,112]{0,1:T(8,128)(2,1)} %collective-permute-done, f32[1024]{0:T(1024)S(1)} %copy-done.10, f32[112]{0:T(128)S(1)} %copy-done.13, ...), kind=kOutput, calls=%fused_computation.91 | convolution fusion | flops 413908992 | bytes 4778176
  185.7 0.6 copy-done.16
  186.4 0.6 gather_fusion
  187.1 0.6 gather_fusion.2
  187.8 0.2 fusion.112
  188.1 2.3 collective-permute-start.7
  190.5 0.8 fusion.79
  191.2 2.1 collective-permute-start.4
  193.5 2.3 fusion
  195.9 2.2 collective-permute-start.1
  198.2 4.3 %collective-permute-start.8 = (bf16[4,2,112]{2,0,1:T(4,128)(2,1)S(1)}, bf16[4,2,112]{2,0,1:T(4,128)(2,1)S(1)}, u32[]{:S(2)}, u32[]{:S(2)}) collective-permute-start(bf16[4,2,112]{2,0,1:T(4,128)(2,1)S(1)} %fusion.88), channel_id=1, source_target_pairs={{0,128},{64,192},{128,0},{192,64},{256,384},{320,448},{384,256},{4... | collective-permute-start | bytes 5384 | tf_op jit(solution)/shard_map/ppermute | solution.py:27
  202.5 1.9 collective-permute-start.5
  204.4 3.6 %collective-permute-start.9 = (bf16[4,2,112]{2,0,1:T(4,128)(2,1)S(1)}, bf16[4,2,112]{2,0,1:T(4,128)(2,1)S(1)}, u32[]{:S(2)}, u32[]{:S(2)}) collective-permute-start(bf16[4,2,112]{2,0,1:T(4,128)(2,1)S(1)} %fusion.90), channel_id=1, source_target_pairs={{0,256},{64,320},{128,384},{192,448},{256,0},{320,64},{384,128},{4... | collective-permute-start | bytes 5384 | tf_op jit(solution)/shard_map/ppermute | solution.py:27
  208.1 3.7 %collective-permute-start.6 = (bf16[4,1,273]{2,0,1:T(4,128)(2,1)S(1)}, bf16[4,1,273]{2,0,1:T(4,128)(2,1)S(1)}, u32[]{:S(2)}, u32[]{:S(2)}) collective-permute-start(bf16[4,1,273]{2,0,1:T(4,128)(2,1)S(1)} %fusion.87), channel_id=1, source_target_pairs={{0,256},{64,320},{128,384},{192,448},{256,0},{320,64},{384,128},{4... | collective-permute-start | bytes 6560 | tf_op jit(solution)/shard_map/ppermute | solution.py:27
  211.9 3.9 %collective-permute-start.2 = (bf16[1,4,273,112]{3,2,1,0:T(8,128)(2,1)S(1)}, bf16[1,4,273,112]{3,2,1,0:T(8,128)(2,1)S(1)}, u32[]{:S(2)}, u32[]{:S(2)}) collective-permute-start(bf16[1,4,273,112]{3,2,1,0:T(8,128)(2,1)S(1)} %fusion.72), channel_id=1, source_target_pairs={{0,128},{64,192},{128,0},{192,64},{256,384},{320,448},{384,256},{4... | collective-permute-start | bytes 733832 | tf_op jit(solution)/shard_map/ppermute | solution.py:27
  215.9 0.6 gather_fusion.4
  216.4 0.7 select_convert_fusion
  217.1 4.8 %collective-permute-done.2 = bf16[1,4,273,112]{3,2,1,0:T(8,128)(2,1)S(1)} collective-permute-done((bf16[1,4,273,112]{3,2,1,0:T(8,128)(2,1)S(1)}, bf16[1,4,273,112]{3,2,1,0:T(8,128)(2,1)S(1)}, u32[]{:S(2)}, u32[]{:S(2)}) %collective-permute-start.2) | collective-permute-done | bytes 244640 | tf_op jit(solution)/shard_map/ppermute | solution.py:27
  222.0 3.3 %collective-permute-start.3 = (bf16[1,4,273,112]{3,2,1,0:T(8,128)(2,1)S(1)}, bf16[1,4,273,112]{3,2,1,0:T(8,128)(2,1)S(1)}, u32[]{:S(2)}, u32[]{:S(2)}) collective-permute-start(bf16[1,4,273,112]{3,2,1,0:T(8,128)(2,1)S(1)} %fusion.51), channel_id=1, source_target_pairs={{0,256},{64,320},{128,384},{192,448},{256,0},{320,64},{384,128},{4... | collective-permute-start | bytes 733832 | tf_op jit(solution)/shard_map/ppermute | solution.py:27
  225.3 0.6 gather_fusion.3
  226.0 0.6 copy.39
  226.6 6.1 %collective-permute-done.3 = bf16[1,4,273,112]{3,2,1,0:T(8,128)(2,1)S(1)} collective-permute-done((bf16[1,4,273,112]{3,2,1,0:T(8,128)(2,1)S(1)}, bf16[1,4,273,112]{3,2,1,0:T(8,128)(2,1)S(1)}, u32[]{:S(2)}, u32[]{:S(2)}) %collective-permute-start.3) | collective-permute-done | bytes 244640 | tf_op jit(solution)/shard_map/ppermute | solution.py:27
  232.8 0.6 gather_fusion.1
  233.5 1.4 copy.38
  234.9 27.8 %reduce-scatter.2.cloned.1.call-done = bf16[1,1024,112]{1,2,0:T(8,128)(2,1)} async-done(((bf16[16,1024,112]{1,2,0:T(8,128)(2,1)}), bf16[1,1024,112]{1,2,0:T(8,128)(2,1)}) %reduce-scatter.2.cloned.1.call-update) | async-done | bytes 229392 | tf_op jit(solution)/shard_map/reduce_scatter | solution.py:184
  (93 shorter events, 1.9 us)
Async XLA Ops:
  7.2 80.2 %copy-start = (bf16[1792,256]{1,0:T(8,128)(2,1)S(1)}, bf16[1792,256]{1,0:T(8,128)(2,1)}, u32[]{:S(2)}) copy-start(bf16[1792,256]{1,0:T(8,128)(2,1)} %param.9) | copy-start | bytes 2752516
  7.2 80.2 %all-gather.7.cloned.1.call-start = ((), (), s32[]{:S(2)}) async-start(), calls=%async_computation.2 | async-start | bytes 1949696 | tf_op jit(solution)/shard_map/all_gather | solution.py:81
  9.0 150.1 %all-gather.5.cloned.1.call-start = ((), (), s32[]{:S(2)}) async-start(), calls=%async_computation.1 | async-start | bytes 1949696 | tf_op jit(solution)/shard_map/all_gather | solution.py:81
  9.7 253.0 %reduce-scatter.2.cloned.1.call-start = ((), (), s32[]{:S(2)}) async-start(), calls=%async_computation.3 | async-start | bytes 3899392 | tf_op jit(solution)/shard_map/reduce_scatter | solution.py:184
  11.4 150.7 %copy-start.7 = (f32[273]{0:T(512)}, f32[273]{0:T(512)S(1)}, u32[]{:S(2)}) copy-start(f32[273]{0:T(512)S(1)} %pad.11.clone) | copy-start | bytes 3280
  11.4 4.7 %copy-start.3 = (s32[1024]{0:T(1024)}, s32[1024]{0:T(1024)S(1)}, u32[]{:S(2)}) copy-start(s32[1024]{0:T(1024)S(1)} %iota_add_fusion.1) | copy-start | bytes 12292
  11.5 5.8 %copy-start.5 = (s32[1024]{0:T(1024)}, s32[1024]{0:T(1024)S(1)}, u32[]{:S(2)}) copy-start(s32[1024]{0:T(1024)S(1)} %convert_reduce_fusion.1) | copy-start | bytes 12292
  90.2 91.3 %collective-permute-start = (bf16[2,112]{0,1:T(8,128)(2,1)}, bf16[2,112]{0,1:T(8,128)(2,1)}, u32[]{:S(2)}, u32[]{:S(2)}) collective-permute-start(bf16[2,112]{0,1:T(8,128)(2,1)} %slice_bitcast_fusion.9), channel_id=1, source_target_pairs={{0,64},{64,128},{128,192},{192,256},{256,320},{320,384},{384,448},... | collective-permute-start | bytes 1352 | tf_op jit(solution)/shard_map/ppermute | solution.py:18
  178.3 3.2 %copy-start.2 = (bf16[112,1792]{1,0:T(8,128)(2,1)S(1)}, bf16[112,1792]{1,0:T(8,128)(2,1)}, u32[]{:S(2)}) copy-start(bf16[112,1792]{1,0:T(8,128)(2,1)} %param.12) | copy-start | bytes 1204228
  178.3 3.3 %copy-start.9 = (f32[1024]{0:T(1024)S(1)}, f32[1024]{0:T(1024)}, u32[]{:S(2)}) copy-start(f32[1024]{0:T(1024)} %get-tuple-element.34) | copy-start | bytes 12292
  178.3 3.3 %copy-start.10 = (f32[1024]{0:T(1024)S(1)}, f32[1024]{0:T(1024)}, u32[]{:S(2)}) copy-start(f32[1024]{0:T(1024)} %get-tuple-element.35) | copy-start | bytes 12292
  178.3 3.3 %copy-start.11 = (f32[1024]{0:T(1024)S(1)}, f32[1024]{0:T(1024)}, u32[]{:S(2)}) copy-start(f32[1024]{0:T(1024)} %get-tuple-element.36) | copy-start | bytes 12292
  178.3 3.3 %copy-start.12 = (f32[112]{0:T(128)S(1)}, f32[112]{0:T(128)}, u32[]{:S(2)}) copy-start(f32[112]{0:T(128)} %get-tuple-element.45) | copy-start | bytes 1348
  178.3 3.3 %copy-start.13 = (f32[112]{0:T(128)S(1)}, f32[112]{0:T(128)}, u32[]{:S(2)}) copy-start(f32[112]{0:T(128)} %get-tuple-element.46) | copy-start | bytes 1348
  178.3 3.3 %copy-start.14 = (f32[112]{0:T(128)S(1)}, f32[112]{0:T(128)}, u32[]{:S(2)}) copy-start(f32[112]{0:T(128)} %get-tuple-element.47) | copy-start | bytes 1348
  178.4 3.3 %copy-start.15 = (f32[112]{0:T(128)S(1)}, f32[112]{0:T(128)}, u32[]{:S(2)}) copy-start(f32[112]{0:T(128)} %param.11) | copy-start | bytes 1348
  185.6 0.7 copy-start.16
  185.6 0.7 copy-start.1
  185.6 1.5 copy-start.17
  185.6 2.1 copy-start.19
  185.6 2.1 copy-start.18
  185.6 2.2 copy-start.6
  185.7 2.2 copy-start.4
  185.7 4.8 %copy-start.8 = (f32[273]{0:T(512)S(1)}, f32[273]{0:T(512)}, u32[]{:S(2)}) copy-start(f32[273]{0:T(512)} %copy-done.7) | copy-start | bytes 3280
  188.1 10.1 %collective-permute-start.7 = (bf16[4,2,112]{2,0,1:T(4,128)(2,1)S(1)}, bf16[4,2,112]{2,0,1:T(4,128)(2,1)S(1)}, u32[]{:S(2)}, u32[]{:S(2)}) collective-permute-start(bf16[4,2,112]{2,0,1:T(4,128)(2,1)S(1)} %get-tuple-element.53), channel_id=1, source_target_pairs={{0,64},{64,0},{128,192},{192,128},{256,320},{320,256},{384,448},{4... | collective-permute-start | bytes 5384 | tf_op jit(solution)/shard_map/ppermute | solution.py:27
  191.2 11.2 %collective-permute-start.4 = (bf16[4,1,273]{2,0,1:T(4,128)(2,1)S(1)}, bf16[4,1,273]{2,0,1:T(4,128)(2,1)S(1)}, u32[]{:S(2)}, u32[]{:S(2)}) collective-permute-start(bf16[4,1,273]{2,0,1:T(4,128)(2,1)S(1)} %convert_bitcast_fusion.3), channel_id=1, source_target_pairs={{0,64},{64,0},{128,192},{192,128},{256,320},{320,256},{384,448},{4... | collective-permute-start | bytes 6560 | tf_op jit(solution)/shard_map/ppermute | solution.py:27
  195.9 16.0 %collective-permute-start.1 = (bf16[1,4,273,112]{3,2,1,0:T(8,128)(2,1)S(1)}, bf16[1,4,273,112]{3,2,1,0:T(8,128)(2,1)S(1)}, u32[]{:S(2)}, u32[]{:S(2)}) collective-permute-start(bf16[1,4,273,112]{3,2,1,0:T(8,128)(2,1)S(1)} %convert_bitcast_fusion), channel_id=1, source_target_pairs={{0,64},{64,0},{128,192},{192,128},{256,320},{320,256},{384,448},{4... | collective-permute-start | bytes 733832 | tf_op jit(solution)/shard_map/ppermute | solution.py:27
  198.2 6.3 %collective-permute-start.8 = (bf16[4,2,112]{2,0,1:T(4,128)(2,1)S(1)}, bf16[4,2,112]{2,0,1:T(4,128)(2,1)S(1)}, u32[]{:S(2)}, u32[]{:S(2)}) collective-permute-start(bf16[4,2,112]{2,0,1:T(4,128)(2,1)S(1)} %fusion.88), channel_id=1, source_target_pairs={{0,128},{64,192},{128,0},{192,64},{256,384},{320,448},{384,256},{4... | collective-permute-start | bytes 5384 | tf_op jit(solution)/shard_map/ppermute | solution.py:27
  202.5 5.6 %collective-permute-start.5 = (bf16[4,1,273]{2,0,1:T(4,128)(2,1)S(1)}, bf16[4,1,273]{2,0,1:T(4,128)(2,1)S(1)}, u32[]{:S(2)}, u32[]{:S(2)}) collective-permute-start(bf16[4,1,273]{2,0,1:T(4,128)(2,1)S(1)} %fusion.89), channel_id=1, source_target_pairs={{0,128},{64,192},{128,0},{192,64},{256,384},{320,448},{384,256},{4... | collective-permute-start | bytes 6560 | tf_op jit(solution)/shard_map/ppermute | solution.py:27
  204.4 11.4 %collective-permute-start.9 = (bf16[4,2,112]{2,0,1:T(4,128)(2,1)S(1)}, bf16[4,2,112]{2,0,1:T(4,128)(2,1)S(1)}, u32[]{:S(2)}, u32[]{:S(2)}) collective-permute-start(bf16[4,2,112]{2,0,1:T(4,128)(2,1)S(1)} %fusion.90), channel_id=1, source_target_pairs={{0,256},{64,320},{128,384},{192,448},{256,0},{320,64},{384,128},{4... | collective-permute-start | bytes 5384 | tf_op jit(solution)/shard_map/ppermute | solution.py:27
  208.1 17.2 %collective-permute-start.6 = (bf16[4,1,273]{2,0,1:T(4,128)(2,1)S(1)}, bf16[4,1,273]{2,0,1:T(4,128)(2,1)S(1)}, u32[]{:S(2)}, u32[]{:S(2)}) collective-permute-start(bf16[4,1,273]{2,0,1:T(4,128)(2,1)S(1)} %fusion.87), channel_id=1, source_target_pairs={{0,256},{64,320},{128,384},{192,448},{256,0},{320,64},{384,128},{4... | collective-permute-start | bytes 6560 | tf_op jit(solution)/shard_map/ppermute | solution.py:27
  211.9 10.0 %collective-permute-start.2 = (bf16[1,4,273,112]{3,2,1,0:T(8,128)(2,1)S(1)}, bf16[1,4,273,112]{3,2,1,0:T(8,128)(2,1)S(1)}, u32[]{:S(2)}, u32[]{:S(2)}) collective-permute-start(bf16[1,4,273,112]{3,2,1,0:T(8,128)(2,1)S(1)} %fusion.72), channel_id=1, source_target_pairs={{0,128},{64,192},{128,0},{192,64},{256,384},{320,448},{384,256},{4... | collective-permute-start | bytes 733832 | tf_op jit(solution)/shard_map/ppermute | solution.py:27
  222.0 10.7 %collective-permute-start.3 = (bf16[1,4,273,112]{3,2,1,0:T(8,128)(2,1)S(1)}, bf16[1,4,273,112]{3,2,1,0:T(8,128)(2,1)S(1)}, u32[]{:S(2)}, u32[]{:S(2)}) collective-permute-start(bf16[1,4,273,112]{3,2,1,0:T(8,128)(2,1)S(1)} %fusion.51), channel_id=1, source_target_pairs={{0,256},{64,320},{128,384},{192,448},{256,0},{320,64},{384,128},{4... | collective-permute-start | bytes 733832 | tf_op jit(solution)/shard_map/ppermute | solution.py:27
Sparse Core Ops, SparseCore 0:
  10.6 76.6 all-gather.6
  90.0 68.9 all-gather.4
  185.8 76.8 reduce-scatter.1
where the time goes:
time: 270 us; the launch traced here: 269 us
  waiting for transfers between devices  174 us (64%)
  starting transfers between devices  29.5 us (11%)
  matrix products  18.6 us (7%)
  between operations  14.4 us (5%)
  blocking collectives  12 us (4%)
  local copies, waits for them, and re-layouts  11.3 us (4%)
  other arithmetic  9.19 us (3%)
    all_gather x2, waiting for transfers between devices, local(): lax.all_gather(part, 'tp', axis=1, tiled=True)  135 us
    reduce_scatter x1, waiting for transfers between devices, local(): summed = lax.psum_scatter(product, 'tp', scatter_dimension=0, tiled=True)  27.8 us
    ppermute x9, starting transfers between devices, psum_doubling(): lax.ppermute(tuple((t.astype(jnp.bfloat16) for t in total)), axis, pairs)  27.4 us
    all_gather x1, blocking collectives, local(): lax.all_gather(tail_state.astype(jnp.bfloat16), 'seq').astype(jnp.float32)  12 us
    ppermute x9, waiting for transfers between devices, psum_doubling(): lax.ppermute(tuple((t.astype(jnp.bfloat16) for t in total)), axis, pairs)  10.9 us
  transfers between devices with their start and end apart: 13, of which 5 were waited for; matrix products, arithmetic and copies ran while one was open for 12% of the time, Pallas kernels for 0%

commit v1 on v0

--- a/solution.py
+++ b/solution.py
@@ -10,6 +10,28 @@
 SLOTS = 4
 EPS = 1e-05
 HIGH = lax.Precision.HIGHEST
+
+
+def in_order(blocks, dim):
+    shape = list(blocks.shape[1:])
+    shape[dim] *= blocks.shape[0]
+    return jnp.moveaxis(blocks, 0, dim).reshape(shape)
+
+
+def collect(value, axis, dim):
+    size = lax.axis_size(axis)
+    pairs = [(i, (i + 1) % size) for i in range(size)]
+    back = [(b, a) for a, b in pairs]
+    lower, upper = ([], [])
+    for step in range(size - 1):
+        if step % 2 == 0:
+            lower.append(lax.ppermute(lower[-1] if lower else value, axis, pairs))
+        else:
+            upper.append(lax.ppermute(upper[-1] if upper else value, axis, back))
+    blocks = jnp.stack([*lower[::-1], value, *upper])
+    shift = lax.axis_index(axis) - len(lower)
+    blocks = blocks[(jnp.arange(size) - shift) % size]
+    return in_order(blocks, dim)
 
 
 def passed_along(shard, axis, by):
@@ -77,9 +99,7 @@
     seg = segment_ids(positions, ends)
     half = tok_rows // 2
     proj_halves = [
-        jnp.dot(
-            lax.all_gather(part, "tp", axis=1, tiled=True), w_in, preferred_element_type=jnp.float32
-        )
+        jnp.dot(collect(part, "tp", 1), w_in, preferred_element_type=jnp.float32)
         .astype(jnp.bfloat16)
         .reshape(half, local_heads, width)
         for part in (tokens[:half], tokens[half:])

time: 270 us -> 261 us (0.967)
  the two profiles are of different devices: /device:TPU:4 before, /device:TPU:10 now
where the time goes in v1:
time: 261 us; the launch traced here: 260 us
  starting transfers between devices  130 us (50%)
  waiting for transfers between devices  49.1 us (19%)
  local copies, waits for them, and re-layouts  26.5 us (10%)
  matrix products  16.4 us (6%)
  between operations  15.2 us (6%)
  blocking collectives  13.2 us (5%)
  other arithmetic  9.08 us (3%)
    ppermute x14, starting transfers between devices, collect(): upper.append(lax.ppermute(upper[-1] if upper else value, axis, back))  57 us
    ppermute x16, starting transfers between devices, collect(): lower.append(lax.ppermute(lower[-1] if lower else value, axis, pairs))  44.6 us
    reduce_scatter x1, waiting for transfers between devices, local(): summed = lax.psum_scatter(product, 'tp', scatter_dimension=0, tiled=True)  28.6 us
    ppermute x9, starting transfers between devices, psum_doubling(): lax.ppermute(tuple((t.astype(jnp.bfloat16) for t in total)), axis, pairs)  26.3 us
    all_gather x1, blocking collectives, local(): lax.all_gather(tail_state.astype(jnp.bfloat16), 'seq').astype(jnp.float32)  13.2 us
    unnamed x77, local copies, waits for them, and re-layouts  12.6 us
    ppermute x9, waiting for transfers between devices, psum_doubling(): lax.ppermute(tuple((t.astype(jnp.bfloat16) for t in total)), axis, pairs)  11.6 us
    ppermute x16, waiting for transfers between devices, collect(): lower.append(lax.ppermute(lower[-1] if lower else value, axis, pairs))  5.91 us
  transfers between devices with their start and end apart: 41, of which 6 were waited for; matrix products, arithmetic and copies ran while one was open for 13% of the time, Pallas kernels for 0%

profile of v1, /device:TPU:10, one launch (start us, length us, event | category | flops | bytes accessed | tf_op | source)
XLA Modules:
  0.0 259.7 jit_solution(9179628633003095533)
XLA Ops:
  8.3 3.8 %collective-permute-start = (bf16[512,112]{0,1:T(8,128)(2,1)S(1)}, bf16[512,112]{0,1:T(8,128)(2,1)S(1)}, u32[]{:S(2)}, u32[]{:S(2)}) collective-permute-start(bf16[512,112]{0,1:T(8,128)(2,1)S(1)} %get-tuple-element.30), channel_id=1, source_target_pairs={{0,4},{4,8},{8,12},{12,16},{16,20},{20,24},{24,28},{28,32},{32,36}... | collective-permute-start | bytes 344072 | tf_op jit(solution)/shard_map/ppermute | solution.py:28
  12.1 9.5 %collective-permute-start.8 = (bf16[512,112]{0,1:T(8,128)(2,1)S(1)}, bf16[512,112]{0,1:T(8,128)(2,1)S(1)}, u32[]{:S(2)}, u32[]{:S(2)}) collective-permute-start(bf16[512,112]{0,1:T(8,128)(2,1)S(1)} %get-tuple-element.30), channel_id=1, source_target_pairs={{4,0},{8,4},{12,8},{16,12},{20,16},{24,20},{28,24},{32,28},{36,32}... | collective-permute-start | bytes 344072 | tf_op jit(solution)/shard_map/ppermute | solution.py:30
  21.6 1.9 collective-permute-start.15
  23.5 5.1 %collective-permute-start.23 = (bf16[512,112]{0,1:T(8,128)(2,1)S(1)}, bf16[512,112]{0,1:T(8,128)(2,1)S(1)}, u32[]{:S(2)}, u32[]{:S(2)}) collective-permute-start(bf16[512,112]{0,1:T(8,128)(2,1)S(1)} %get-tuple-element.31), channel_id=1, source_target_pairs={{4,0},{8,4},{12,8},{16,12},{20,16},{24,20},{28,24},{32,28},{36,32}... | collective-permute-start | bytes 344072 | tf_op jit(solution)/shard_map/ppermute | solution.py:30
  32.3 1.9 collective-permute-start.16
  34.2 2.0 fusion.84
  38.1 2.1 collective-permute-done.16
  42.7 5.1 %collective-permute-start.9 = (bf16[512,112]{0,1:T(8,128)(2,1)S(1)}, bf16[512,112]{0,1:T(8,128)(2,1)S(1)}, u32[]{:S(2)}, u32[]{:S(2)}) collective-permute-start(bf16[512,112]{0,1:T(8,128)(2,1)S(1)} %collective-permute-done.8), channel_id=1, source_target_pairs={{4,0},{8,4},{12,8},{16,12},{20,16},{24,20},{28,24},{32,28},{36,32}... | collective-permute-start | bytes 344072 | tf_op jit(solution)/shard_map/ppermute | solution.py:30
  47.9 1.9 collective-permute-start.24
  49.8 3.9 %collective-permute-start.2 = (bf16[512,112]{0,1:T(8,128)(2,1)S(1)}, bf16[512,112]{0,1:T(8,128)(2,1)S(1)}, u32[]{:S(2)}, u32[]{:S(2)}) collective-permute-start(bf16[512,112]{0,1:T(8,128)(2,1)S(1)} %collective-permute-done.1), channel_id=1, source_target_pairs={{0,4},{4,8},{8,12},{12,16},{16,20},{20,24},{24,28},{28,32},{32,36}... | collective-permute-start | bytes 344072 | tf_op jit(solution)/shard_map/ppermute | solution.py:28
  53.7 1.9 collective-permute-start.18
  56.3 5.1 %collective-permute-start.10 = (bf16[512,112]{0,1:T(8,128)(2,1)S(1)}, bf16[512,112]{0,1:T(8,128)(2,1)S(1)}, u32[]{:S(2)}, u32[]{:S(2)}) collective-permute-start(bf16[512,112]{0,1:T(8,128)(2,1)S(1)} %collective-permute-done.9), channel_id=1, source_target_pairs={{4,0},{8,4},{12,8},{16,12},{20,16},{24,20},{28,24},{32,28},{36,32}... | collective-permute-start | bytes 344072 | tf_op jit(solution)/shard_map/ppermute | solution.py:30
  61.4 1.9 collective-permute-start.25
  63.3 3.9 %collective-permute-start.3 = (bf16[512,112]{0,1:T(8,128)(2,1)S(1)}, bf16[512,112]{0,1:T(8,128)(2,1)S(1)}, u32[]{:S(2)}, u32[]{:S(2)}) collective-permute-start(bf16[512,112]{0,1:T(8,128)(2,1)S(1)} %collective-permute-done.2), channel_id=1, source_target_pairs={{0,4},{4,8},{8,12},{12,16},{16,20},{20,24},{24,28},{28,32},{32,36}... | collective-permute-start | bytes 344072 | tf_op jit(solution)/shard_map/ppermute | solution.py:28
  67.3 1.9 collective-permute-start.19
  69.2 5.1 %collective-permute-start.11 = (bf16[512,112]{0,1:T(8,128)(2,1)S(1)}, bf16[512,112]{0,1:T(8,128)(2,1)S(1)}, u32[]{:S(2)}, u32[]{:S(2)}) collective-permute-start(bf16[512,112]{0,1:T(8,128)(2,1)S(1)} %collective-permute-done.10), channel_id=1, source_target_pairs={{4,0},{8,4},{12,8},{16,12},{20,16},{24,20},{28,24},{32,28},{36,32}... | collective-permute-start | bytes 344072 | tf_op jit(solution)/shard_map/ppermute | solution.py:30
  74.4 1.9 collective-permute-start.26
  76.3 3.9 %collective-permute-start.4 = (bf16[512,112]{0,1:T(8,128)(2,1)S(1)}, bf16[512,112]{0,1:T(8,128)(2,1)S(1)}, u32[]{:S(2)}, u32[]{:S(2)}) collective-permute-start(bf16[512,112]{0,1:T(8,128)(2,1)S(1)} %collective-permute-done.3), channel_id=1, source_target_pairs={{0,4},{4,8},{8,12},{12,16},{16,20},{20,24},{24,28},{28,32},{32,36}... | collective-permute-start | bytes 344072 | tf_op jit(solution)/shard_map/ppermute | solution.py:28
  80.3 1.9 collective-permute-start.20
  83.6 5.1 %collective-permute-start.12 = (bf16[512,112]{0,1:T(8,128)(2,1)S(1)}, bf16[512,112]{0,1:T(8,128)(2,1)S(1)}, u32[]{:S(2)}, u32[]{:S(2)}) collective-permute-start(bf16[512,112]{0,1:T(8,128)(2,1)S(1)} %collective-permute-done.11), channel_id=1, source_target_pairs={{4,0},{8,4},{12,8},{16,12},{20,16},{24,20},{28,24},{32,28},{36,32}... | collective-permute-start | bytes 344072 | tf_op jit(solution)/shard_map/ppermute | solution.py:30
  88.7 1.9 collective-permute-start.27
  90.6 3.9 %collective-permute-start.5 = (bf16[512,112]{0,1:T(8,128)(2,1)S(1)}, bf16[512,112]{0,1:T(8,128)(2,1)S(1)}, u32[]{:S(2)}, u32[]{:S(2)}) collective-permute-start(bf16[512,112]{0,1:T(8,128)(2,1)S(1)} %collective-permute-done.4), channel_id=1, source_target_pairs={{0,4},{4,8},{8,12},{12,16},{16,20},{20,24},{24,28},{28,32},{32,36}... | collective-permute-start | bytes 344072 | tf_op jit(solution)/shard_map/ppermute | solution.py:28
  94.6 1.9 collective-permute-start.21
  97.7 5.1 %collective-permute-start.13 = (bf16[512,112]{0,1:T(8,128)(2,1)S(1)}, bf16[512,112]{0,1:T(8,128)(2,1)S(1)}, u32[]{:S(2)}, u32[]{:S(2)}) collective-permute-start(bf16[512,112]{0,1:T(8,128)(2,1)S(1)} %collective-permute-done.12), channel_id=1, source_target_pairs={{4,0},{8,4},{12,8},{16,12},{20,16},{24,20},{28,24},{32,28},{36,32}... | collective-permute-start | bytes 344072 | tf_op jit(solution)/shard_map/ppermute | solution.py:30
  102.8 1.9 collective-permute-start.28
  104.8 3.9 %collective-permute-start.6 = (bf16[512,112]{0,1:T(8,128)(2,1)S(1)}, bf16[512,112]{0,1:T(8,128)(2,1)S(1)}, u32[]{:S(2)}, u32[]{:S(2)}) collective-permute-start(bf16[512,112]{0,1:T(8,128)(2,1)S(1)} %collective-permute-done.5), channel_id=1, source_target_pairs={{0,4},{4,8},{8,12},{12,16},{16,20},{20,24},{24,28},{28,32},{32,36}... | collective-permute-start | bytes 344072 | tf_op jit(solution)/shard_map/ppermute | solution.py:28
  110.7 5.3 %collective-permute-start.14 = (bf16[512,112]{0,1:T(8,128)(2,1)S(1)}, bf16[512,112]{0,1:T(8,128)(2,1)S(1)}, u32[]{:S(2)}, u32[]{:S(2)}) collective-permute-start(bf16[512,112]{0,1:T(8,128)(2,1)S(1)} %collective-permute-done.13), channel_id=1, source_target_pairs={{4,0},{8,4},{12,8},{16,12},{20,16},{24,20},{28,24},{32,28},{36,32}... | collective-permute-start | bytes 344072 | tf_op jit(solution)/shard_map/ppermute | solution.py:30
  117.9 3.9 %collective-permute-start.7 = (bf16[512,112]{0,1:T(8,128)(2,1)S(1)}, bf16[512,112]{0,1:T(8,128)(2,1)S(1)}, u32[]{:S(2)}, u32[]{:S(2)}) collective-permute-start(bf16[512,112]{0,1:T(8,128)(2,1)S(1)} %collective-permute-done.6), channel_id=1, source_target_pairs={{0,4},{4,8},{8,12},{12,16},{16,20},{20,24},{24,28},{28,32},{32,36}... | collective-permute-start | bytes 344072 | tf_op jit(solution)/shard_map/ppermute | solution.py:28
  122.0 3.8 %collective-permute-done.7 = bf16[512,112]{0,1:T(8,128)(2,1)S(1)} collective-permute-done((bf16[512,112]{0,1:T(8,128)(2,1)S(1)}, bf16[512,112]{0,1:T(8,128)(2,1)S(1)}, u32[]{:S(2)}, u32[]{:S(2)}) %collective-permute-start.7) | collective-permute-done | bytes 114720 | tf_op jit(solution)/shard_map/ppermute | solution.py:28
  136.4 3.4 %gather_fusion = bf16[16,512,112]{1,2,0:T(8,128)(2,1)} fusion(bf16[16,512,112]{1,2,0:T(8,128)(2,1)} %bitcast_dynamic-update-slice_fusion.16, s32[1024]{0:T(1024)S(1)} %pad_clamp_fusion.2), kind=kCustom, calls=%fused_computation | custom fusion | bytes 3670080 | tf_op jit(solution)/shard_map/gather | solution.py:33
  141.8 2.3 fusion.11
  146.7 13.2 %all-gather.1 = bf16[8,273,112]{2,1,0:T(8,128)(2,1)S(1)} all-gather(bf16[1,273,112]{2,1,0:T(8,128)(2,1)S(1)} %fusion.19), channel_id=2, replica_groups=mesh['seq'=8,'tp'=16,'req'=4] {'seq'}, dimensions={0}, use_global_device_ids=true | all-gather | bytes 550368 | tf_op jit(solution)/shard_map/all_gather | solution.py:183
  161.5 2.3 fusion.13
  164.8 2.2 multiply_reduce_fusion
  167.0 2.3 collective-permute-start.30
  169.3 2.9 %collective-permute-done.30 = bf16[2,112]{0,1:T(8,128)(2,1)S(1)} collective-permute-done((bf16[2,112]{0,1:T(8,128)(2,1)S(1)}, bf16[2,112]{0,1:T(8,128)(2,1)S(1)}, u32[]{:S(2)}, u32[]{:S(2)}) %collective-permute-start.30) | collective-permute-done | bytes 480 | tf_op jit(solution)/shard_map/ppermute | solution.py:40
  172.2 3.2 %fusion.60 = bf16[1024,1792]{0,1} fusion(bf16[112,1792]{1,0:T(8,128)(2,1)S(1)} %copy-done.3, bf16[1024,112]{0,1:T(8,128)(2,1)S(1)} %fusion.94, f32[1024,1,112]{0,2,1:T(8,128)S(1)} %get-tuple-element.54, bf16[2,112]{0,1:T(8,128)(2,1)S(1)} %collective-permute-done.30, f32[1024]{0:T(1024)S(1)} %copy-done.13, f32[112]{0:T(128)S(1)} %copy-done.16, ...), kind=kOutput, calls=%fused_computation.93 | convolution fusion | flops 413908992 | bytes 4778176
  177.8 1.9 collective-permute-start.37
  180.7 2.6 %collective-permute-start.34 = (bf16[4,1,273]{2,0,1:T(4,128)(2,1)S(1)}, bf16[4,1,273]{2,0,1:T(4,128)(2,1)S(1)}, u32[]{:S(2)}, u32[]{:S(2)}) collective-permute-start(bf16[4,1,273]{2,0,1:T(4,128)(2,1)S(1)} %convert_bitcast_fusion.3), channel_id=1, source_target_pairs={{0,64},{64,0},{128,192},{192,128},{256,320},{320,256},{384,448},{4... | collective-permute-start | bytes 6560 | tf_op jit(solution)/shard_map/ppermute | solution.py:49
  183.5 2.3 fusion
  189.8 3.9 %collective-permute-start.35 = (bf16[4,1,273]{2,0,1:T(4,128)(2,1)S(1)}, bf16[4,1,273]{2,0,1:T(4,128)(2,1)S(1)}, u32[]{:S(2)}, u32[]{:S(2)}) collective-permute-start(bf16[4,1,273]{2,0,1:T(4,128)(2,1)S(1)} %fusion.89), channel_id=1, source_target_pairs={{0,128},{64,192},{128,0},{192,64},{256,384},{320,448},{384,256},{4... | collective-permute-start | bytes 6560 | tf_op jit(solution)/shard_map/ppermute | solution.py:49
  193.7 4.0 %collective-permute-start.39 = (bf16[4,2,112]{2,0,1:T(4,128)(2,1)S(1)}, bf16[4,2,112]{2,0,1:T(4,128)(2,1)S(1)}, u32[]{:S(2)}, u32[]{:S(2)}) collective-permute-start(bf16[4,2,112]{2,0,1:T(4,128)(2,1)S(1)} %fusion.90), channel_id=1, source_target_pairs={{0,256},{64,320},{128,384},{192,448},{256,0},{320,64},{384,128},{4... | collective-permute-start | bytes 5384 | tf_op jit(solution)/shard_map/ppermute | solution.py:49
  197.7 3.4 %collective-permute-start.36 = (bf16[4,1,273]{2,0,1:T(4,128)(2,1)S(1)}, bf16[4,1,273]{2,0,1:T(4,128)(2,1)S(1)}, u32[]{:S(2)}, u32[]{:S(2)}) collective-permute-start(bf16[4,1,273]{2,0,1:T(4,128)(2,1)S(1)} %fusion.87), channel_id=1, source_target_pairs={{0,256},{64,320},{128,384},{192,448},{256,0},{320,64},{384,128},{4... | collective-permute-start | bytes 6560 | tf_op jit(solution)/shard_map/ppermute | solution.py:49
  201.2 2.6 %collective-permute-start.32 = (bf16[1,4,273,112]{3,2,1,0:T(8,128)(2,1)S(1)}, bf16[1,4,273,112]{3,2,1,0:T(8,128)(2,1)S(1)}, u32[]{:S(2)}, u32[]{:S(2)}) collective-permute-start(bf16[1,4,273,112]{3,2,1,0:T(8,128)(2,1)S(1)} %fusion.72), channel_id=1, source_target_pairs={{0,128},{64,192},{128,0},{192,64},{256,384},{320,448},{384,256},{4... | collective-permute-start | bytes 733832 | tf_op jit(solution)/shard_map/ppermute | solution.py:49
  205.1 6.1 %collective-permute-done.32 = bf16[1,4,273,112]{3,2,1,0:T(8,128)(2,1)S(1)} collective-permute-done((bf16[1,4,273,112]{3,2,1,0:T(8,128)(2,1)S(1)}, bf16[1,4,273,112]{3,2,1,0:T(8,128)(2,1)S(1)}, u32[]{:S(2)}, u32[]{:S(2)}) %collective-permute-start.32) | collective-permute-done | bytes 244640 | tf_op jit(solution)/shard_map/ppermute | solution.py:49
  211.3 4.0 %collective-permute-start.33 = (bf16[1,4,273,112]{3,2,1,0:T(8,128)(2,1)S(1)}, bf16[1,4,273,112]{3,2,1,0:T(8,128)(2,1)S(1)}, u32[]{:S(2)}, u32[]{:S(2)}) collective-permute-start(bf16[1,4,273,112]{3,2,1,0:T(8,128)(2,1)S(1)} %fusion.51), channel_id=1, source_target_pairs={{0,256},{64,320},{128,384},{192,448},{256,0},{320,64},{384,128},{4... | collective-permute-start | bytes 733832 | tf_op jit(solution)/shard_map/ppermute | solution.py:49
  216.6 5.5 %collective-permute-done.33 = bf16[1,4,273,112]{3,2,1,0:T(8,128)(2,1)S(1)} collective-permute-done((bf16[1,4,273,112]{3,2,1,0:T(8,128)(2,1)S(1)}, bf16[1,4,273,112]{3,2,1,0:T(8,128)(2,1)S(1)}, u32[]{:S(2)}, u32[]{:S(2)}) %collective-permute-start.33) | collective-permute-done | bytes 244640 | tf_op jit(solution)/shard_map/ppermute | solution.py:49
  224.3 28.6 %reduce-scatter.2.cloned.1.call-done = bf16[1,1024,112]{1,2,0:T(8,128)(2,1)} async-done(((bf16[16,1024,112]{1,2,0:T(8,128)(2,1)}), bf16[1,1024,112]{1,2,0:T(8,128)(2,1)}) %reduce-scatter.2.cloned.1.call-update) | async-done | bytes 229392 | tf_op jit(solution)/shard_map/reduce_scatter | solution.py:204
  (188 shorter events, 45.9 us)
Async XLA Ops:
  7.2 134.6 %copy-start = (bf16[1792,256]{1,0:T(8,128)(2,1)S(1)}, bf16[1792,256]{1,0:T(8,128)(2,1)}, u32[]{:S(2)}) copy-start(bf16[1792,256]{1,0:T(8,128)(2,1)} %param.9) | copy-start | bytes 2752516
  7.2 245.7 %reduce-scatter.2.cloned.1.call-start = ((), (), s32[]{:S(2)}) async-start(), calls=%async_computation.1 | async-start | bytes 3899392 | tf_op jit(solution)/shard_map/reduce_scatter | solution.py:204
  8.3 27.9 %collective-permute-start = (bf16[512,112]{0,1:T(8,128)(2,1)S(1)}, bf16[512,112]{0,1:T(8,128)(2,1)S(1)}, u32[]{:S(2)}, u32[]{:S(2)}) collective-permute-start(bf16[512,112]{0,1:T(8,128)(2,1)S(1)} %get-tuple-element.30), channel_id=1, source_target_pairs={{0,4},{4,8},{8,12},{12,16},{16,20},{20,24},{24,28},{28,32},{32,36}... | collective-permute-start | bytes 344072 | tf_op jit(solution)/shard_map/ppermute | solution.py:28
  12.1 30.6 %collective-permute-start.8 = (bf16[512,112]{0,1:T(8,128)(2,1)S(1)}, bf16[512,112]{0,1:T(8,128)(2,1)S(1)}, u32[]{:S(2)}, u32[]{:S(2)}) collective-permute-start(bf16[512,112]{0,1:T(8,128)(2,1)S(1)} %get-tuple-element.30), channel_id=1, source_target_pairs={{4,0},{8,4},{12,8},{16,12},{20,16},{24,20},{28,24},{32,28},{36,32}... | collective-permute-start | bytes 344072 | tf_op jit(solution)/shard_map/ppermute | solution.py:30
  21.6 10.7 %collective-permute-start.15 = (bf16[512,112]{0,1:T(8,128)(2,1)S(1)}, bf16[512,112]{0,1:T(8,128)(2,1)S(1)}, u32[]{:S(2)}, u32[]{:S(2)}) collective-permute-start(bf16[512,112]{0,1:T(8,128)(2,1)S(1)} %get-tuple-element.31), channel_id=1, source_target_pairs={{0,4},{4,8},{8,12},{12,16},{16,20},{20,24},{24,28},{28,32},{32,36}... | collective-permute-start | bytes 344072 | tf_op jit(solution)/shard_map/ppermute | solution.py:28
  23.5 24.3 %collective-permute-start.23 = (bf16[512,112]{0,1:T(8,128)(2,1)S(1)}, bf16[512,112]{0,1:T(8,128)(2,1)S(1)}, u32[]{:S(2)}, u32[]{:S(2)}) collective-permute-start(bf16[512,112]{0,1:T(8,128)(2,1)S(1)} %get-tuple-element.31), channel_id=1, source_target_pairs={{4,0},{8,4},{12,8},{16,12},{20,16},{24,20},{28,24},{32,28},{36,32}... | collective-permute-start | bytes 344072 | tf_op jit(solution)/shard_map/ppermute | solution.py:30
  28.7 93.2 %copy-start.5 = (s32[1024]{0:T(1024)}, s32[1024]{0:T(1024)S(1)}, u32[]{:S(2)}) copy-start(s32[1024]{0:T(1024)S(1)} %iota_add_fusion.1) | copy-start | bytes 12292
  31.5 90.4 %copy-start.7 = (s32[1024]{0:T(1024)}, s32[1024]{0:T(1024)S(1)}, u32[]{:S(2)}) copy-start(s32[1024]{0:T(1024)S(1)} %convert_reduce_fusion.1) | copy-start | bytes 12292
  32.3 7.9 %collective-permute-start.16 = (bf16[512,112]{0,1:T(8,128)(2,1)S(1)}, bf16[512,112]{0,1:T(8,128)(2,1)S(1)}, u32[]{:S(2)}, u32[]{:S(2)}) collective-permute-start(bf16[512,112]{0,1:T(8,128)(2,1)S(1)} %collective-permute-done.15), channel_id=1, source_target_pairs={{0,4},{4,8},{8,12},{12,16},{16,20},{20,24},{24,28},{28,32},{32,36}... | collective-permute-start | bytes 344072 | tf_op jit(solution)/shard_map/ppermute | solution.py:28
  36.2 13.6 %collective-permute-start.1 = (bf16[512,112]{0,1:T(8,128)(2,1)S(1)}, bf16[512,112]{0,1:T(8,128)(2,1)S(1)}, u32[]{:S(2)}, u32[]{:S(2)}) collective-permute-start(bf16[512,112]{0,1:T(8,128)(2,1)S(1)} %collective-permute-done), channel_id=1, source_target_pairs={{0,4},{4,8},{8,12},{12,16},{16,20},{20,24},{24,28},{28,32},{32,36}... | collective-permute-start | bytes 344072 | tf_op jit(solution)/shard_map/ppermute | solution.py:28
  40.2 13.5 %collective-permute-start.17 = (bf16[512,112]{0,1:T(8,128)(2,1)S(1)}, bf16[512,112]{0,1:T(8,128)(2,1)S(1)}, u32[]{:S(2)}, u32[]{:S(2)}) collective-permute-start(bf16[512,112]{0,1:T(8,128)(2,1)S(1)} %collective-permute-done.16), channel_id=1, source_target_pairs={{0,4},{4,8},{8,12},{12,16},{16,20},{20,24},{24,28},{28,32},{32,36}... | collective-permute-start | bytes 344072 | tf_op jit(solution)/shard_map/ppermute | solution.py:28
  42.7 13.6 %collective-permute-start.9 = (bf16[512,112]{0,1:T(8,128)(2,1)S(1)}, bf16[512,112]{0,1:T(8,128)(2,1)S(1)}, u32[]{:S(2)}, u32[]{:S(2)}) collective-permute-start(bf16[512,112]{0,1:T(8,128)(2,1)S(1)} %collective-permute-done.8), channel_id=1, source_target_pairs={{4,0},{8,4},{12,8},{16,12},{20,16},{24,20},{28,24},{32,28},{36,32}... | collective-permute-start | bytes 344072 | tf_op jit(solution)/shard_map/ppermute | solution.py:30
  47.9 13.5 %collective-permute-start.24 = (bf16[512,112]{0,1:T(8,128)(2,1)S(1)}, bf16[512,112]{0,1:T(8,128)(2,1)S(1)}, u32[]{:S(2)}, u32[]{:S(2)}) collective-permute-start(bf16[512,112]{0,1:T(8,128)(2,1)S(1)} %collective-permute-done.23), channel_id=1, source_target_pairs={{4,0},{8,4},{12,8},{16,12},{20,16},{24,20},{28,24},{32,28},{36,32}... | collective-permute-start | bytes 344072 | tf_op jit(solution)/shard_map/ppermute | solution.py:30
  49.8 13.5 %collective-permute-start.2 = (bf16[512,112]{0,1:T(8,128)(2,1)S(1)}, bf16[512,112]{0,1:T(8,128)(2,1)S(1)}, u32[]{:S(2)}, u32[]{:S(2)}) collective-permute-start(bf16[512,112]{0,1:T(8,128)(2,1)S(1)} %collective-permute-done.1), channel_id=1, source_target_pairs={{0,4},{4,8},{8,12},{12,16},{16,20},{20,24},{24,28},{28,32},{32,36}... | collective-permute-start | bytes 344072 | tf_op jit(solution)/shard_map/ppermute | solution.py:28
  53.7 13.5 %collective-permute-start.18 = (bf16[512,112]{0,1:T(8,128)(2,1)S(1)}, bf16[512,112]{0,1:T(8,128)(2,1)S(1)}, u32[]{:S(2)}, u32[]{:S(2)}) collective-permute-start(bf16[512,112]{0,1:T(8,128)(2,1)S(1)} %collective-permute-done.17), channel_id=1, source_target_pairs={{0,4},{4,8},{8,12},{12,16},{16,20},{20,24},{24,28},{28,32},{32,36}... | collective-permute-start | bytes 344072 | tf_op jit(solution)/shard_map/ppermute | solution.py:28
  56.3 13.0 %collective-permute-start.10 = (bf16[512,112]{0,1:T(8,128)(2,1)S(1)}, bf16[512,112]{0,1:T(8,128)(2,1)S(1)}, u32[]{:S(2)}, u32[]{:S(2)}) collective-permute-start(bf16[512,112]{0,1:T(8,128)(2,1)S(1)} %collective-permute-done.9), channel_id=1, source_target_pairs={{4,0},{8,4},{12,8},{16,12},{20,16},{24,20},{28,24},{32,28},{36,32}... | collective-permute-start | bytes 344072 | tf_op jit(solution)/shard_map/ppermute | solution.py:30
  61.4 13.0 %collective-permute-start.25 = (bf16[512,112]{0,1:T(8,128)(2,1)S(1)}, bf16[512,112]{0,1:T(8,128)(2,1)S(1)}, u32[]{:S(2)}, u32[]{:S(2)}) collective-permute-start(bf16[512,112]{0,1:T(8,128)(2,1)S(1)} %collective-permute-done.24), channel_id=1, source_target_pairs={{4,0},{8,4},{12,8},{16,12},{20,16},{24,20},{28,24},{32,28},{36,32}... | collective-permute-start | bytes 344072 | tf_op jit(solution)/shard_map/ppermute | solution.py:30
  63.3 13.0 %collective-permute-start.3 = (bf16[512,112]{0,1:T(8,128)(2,1)S(1)}, bf16[512,112]{0,1:T(8,128)(2,1)S(1)}, u32[]{:S(2)}, u32[]{:S(2)}) collective-permute-start(bf16[512,112]{0,1:T(8,128)(2,1)S(1)} %collective-permute-done.2), channel_id=1, source_target_pairs={{0,4},{4,8},{8,12},{12,16},{16,20},{20,24},{24,28},{28,32},{32,36}... | collective-permute-start | bytes 344072 | tf_op jit(solution)/shard_map/ppermute | solution.py:28
  67.3 13.0 %collective-permute-start.19 = (bf16[512,112]{0,1:T(8,128)(2,1)S(1)}, bf16[512,112]{0,1:T(8,128)(2,1)S(1)}, u32[]{:S(2)}, u32[]{:S(2)}) collective-permute-start(bf16[512,112]{0,1:T(8,128)(2,1)S(1)} %collective-permute-done.18), channel_id=1, source_target_pairs={{0,4},{4,8},{8,12},{12,16},{16,20},{20,24},{24,28},{28,32},{32,36}... | collective-permute-start | bytes 344072 | tf_op jit(solution)/shard_map/ppermute | solution.py:28
  69.2 14.3 %collective-permute-start.11 = (bf16[512,112]{0,1:T(8,128)(2,1)S(1)}, bf16[512,112]{0,1:T(8,128)(2,1)S(1)}, u32[]{:S(2)}, u32[]{:S(2)}) collective-permute-start(bf16[512,112]{0,1:T(8,128)(2,1)S(1)} %collective-permute-done.10), channel_id=1, source_target_pairs={{4,0},{8,4},{12,8},{16,12},{20,16},{24,20},{28,24},{32,28},{36,32}... | collective-permute-start | bytes 344072 | tf_op jit(solution)/shard_map/ppermute | solution.py:30
  74.4 14.3 %collective-permute-start.26 = (bf16[512,112]{0,1:T(8,128)(2,1)S(1)}, bf16[512,112]{0,1:T(8,128)(2,1)S(1)}, u32[]{:S(2)}, u32[]{:S(2)}) collective-permute-start(bf16[512,112]{0,1:T(8,128)(2,1)S(1)} %collective-permute-done.25), channel_id=1, source_target_pairs={{4,0},{8,4},{12,8},{16,12},{20,16},{24,20},{28,24},{32,28},{36,32}... | collective-permute-start | bytes 344072 | tf_op jit(solution)/shard_map/ppermute | solution.py:30
  76.3 14.3 %collective-permute-start.4 = (bf16[512,112]{0,1:T(8,128)(2,1)S(1)}, bf16[512,112]{0,1:T(8,128)(2,1)S(1)}, u32[]{:S(2)}, u32[]{:S(2)}) collective-permute-start(bf16[512,112]{0,1:T(8,128)(2,1)S(1)} %collective-permute-done.3), channel_id=1, source_target_pairs={{0,4},{4,8},{8,12},{12,16},{16,20},{20,24},{24,28},{28,32},{32,36}... | collective-permute-start | bytes 344072 | tf_op jit(solution)/shard_map/ppermute | solution.py:28
  80.3 14.3 %collective-permute-start.20 = (bf16[512,112]{0,1:T(8,128)(2,1)S(1)}, bf16[512,112]{0,1:T(8,128)(2,1)S(1)}, u32[]{:S(2)}, u32[]{:S(2)}) collective-permute-start(bf16[512,112]{0,1:T(8,128)(2,1)S(1)} %collective-permute-done.19), channel_id=1, source_target_pairs={{0,4},{4,8},{8,12},{12,16},{16,20},{20,24},{24,28},{28,32},{32,36}... | collective-permute-start | bytes 344072 | tf_op jit(solution)/shard_map/ppermute | solution.py:28
  83.6 14.1 %collective-permute-start.12 = (bf16[512,112]{0,1:T(8,128)(2,1)S(1)}, bf16[512,112]{0,1:T(8,128)(2,1)S(1)}, u32[]{:S(2)}, u32[]{:S(2)}) collective-permute-start(bf16[512,112]{0,1:T(8,128)(2,1)S(1)} %collective-permute-done.11), channel_id=1, source_target_pairs={{4,0},{8,4},{12,8},{16,12},{20,16},{24,20},{28,24},{32,28},{36,32}... | collective-permute-start | bytes 344072 | tf_op jit(solution)/shard_map/ppermute | solution.py:30
  88.7 14.1 %collective-permute-start.27 = (bf16[512,112]{0,1:T(8,128)(2,1)S(1)}, bf16[512,112]{0,1:T(8,128)(2,1)S(1)}, u32[]{:S(2)}, u32[]{:S(2)}) collective-permute-start(bf16[512,112]{0,1:T(8,128)(2,1)S(1)} %collective-permute-done.26), channel_id=1, source_target_pairs={{4,0},{8,4},{12,8},{16,12},{20,16},{24,20},{28,24},{32,28},{36,32}... | collective-permute-start | bytes 344072 | tf_op jit(solution)/shard_map/ppermute | solution.py:30
  90.6 14.1 %collective-permute-start.5 = (bf16[512,112]{0,1:T(8,128)(2,1)S(1)}, bf16[512,112]{0,1:T(8,128)(2,1)S(1)}, u32[]{:S(2)}, u32[]{:S(2)}) collective-permute-start(bf16[512,112]{0,1:T(8,128)(2,1)S(1)} %collective-permute-done.4), channel_id=1, source_target_pairs={{0,4},{4,8},{8,12},{12,16},{16,20},{20,24},{24,28},{28,32},{32,36}... | collective-permute-start | bytes 344072 | tf_op jit(solution)/shard_map/ppermute | solution.py:28
  94.6 14.1 %collective-permute-start.21 = (bf16[512,112]{0,1:T(8,128)(2,1)S(1)}, bf16[512,112]{0,1:T(8,128)(2,1)S(1)}, u32[]{:S(2)}, u32[]{:S(2)}) collective-permute-start(bf16[512,112]{0,1:T(8,128)(2,1)S(1)} %collective-permute-done.20), channel_id=1, source_target_pairs={{0,4},{4,8},{8,12},{12,16},{16,20},{20,24},{24,28},{28,32},{32,36}... | collective-permute-start | bytes 344072 | tf_op jit(solution)/shard_map/ppermute | solution.py:28
  97.7 13.0 %collective-permute-start.13 = (bf16[512,112]{0,1:T(8,128)(2,1)S(1)}, bf16[512,112]{0,1:T(8,128)(2,1)S(1)}, u32[]{:S(2)}, u32[]{:S(2)}) collective-permute-start(bf16[512,112]{0,1:T(8,128)(2,1)S(1)} %collective-permute-done.12), channel_id=1, source_target_pairs={{4,0},{8,4},{12,8},{16,12},{20,16},{24,20},{28,24},{32,28},{36,32}... | collective-permute-start | bytes 344072 | tf_op jit(solution)/shard_map/ppermute | solution.py:30
  102.8 13.2 %collective-permute-start.28 = (bf16[512,112]{0,1:T(8,128)(2,1)S(1)}, bf16[512,112]{0,1:T(8,128)(2,1)S(1)}, u32[]{:S(2)}, u32[]{:S(2)}) collective-permute-start(bf16[512,112]{0,1:T(8,128)(2,1)S(1)} %collective-permute-done.27), channel_id=1, source_target_pairs={{4,0},{8,4},{12,8},{16,12},{20,16},{24,20},{28,24},{32,28},{36,32}... | collective-permute-start | bytes 344072 | tf_op jit(solution)/shard_map/ppermute | solution.py:30
  104.8 13.2 %collective-permute-start.6 = (bf16[512,112]{0,1:T(8,128)(2,1)S(1)}, bf16[512,112]{0,1:T(8,128)(2,1)S(1)}, u32[]{:S(2)}, u32[]{:S(2)}) collective-permute-start(bf16[512,112]{0,1:T(8,128)(2,1)S(1)} %collective-permute-done.5), channel_id=1, source_target_pairs={{0,4},{4,8},{8,12},{12,16},{16,20},{20,24},{24,28},{28,32},{32,36}... | collective-permute-start | bytes 344072 | tf_op jit(solution)/shard_map/ppermute | solution.py:28
  108.7 13.2 %collective-permute-start.22 = (bf16[512,112]{0,1:T(8,128)(2,1)S(1)}, bf16[512,112]{0,1:T(8,128)(2,1)S(1)}, u32[]{:S(2)}, u32[]{:S(2)}) collective-permute-start(bf16[512,112]{0,1:T(8,128)(2,1)S(1)} %collective-permute-done.21), channel_id=1, source_target_pairs={{0,4},{4,8},{8,12},{12,16},{16,20},{20,24},{24,28},{28,32},{32,36}... | collective-permute-start | bytes 344072 | tf_op jit(solution)/shard_map/ppermute | solution.py:28
  110.7 35.5 %copy-start.10 = (f32[273]{0:T(512)}, f32[273]{0:T(512)S(1)}, u32[]{:S(2)}) copy-start(f32[273]{0:T(512)S(1)} %pad.11.clone) | copy-start | bytes 3280
  110.7 20.4 %copy-start.4 = (bf16[1024,112]{0,1:T(8,128)(2,1)S(1)}, bf16[1024,112]{0,1:T(8,128)(2,1)}, u32[]{:S(2)}) copy-start(bf16[1024,112]{0,1:T(8,128)(2,1)} %param.8) | copy-start | bytes 688132
  110.7 25.0 %collective-permute-start.14 = (bf16[512,112]{0,1:T(8,128)(2,1)S(1)}, bf16[512,112]{0,1:T(8,128)(2,1)S(1)}, u32[]{:S(2)}, u32[]{:S(2)}) collective-permute-start(bf16[512,112]{0,1:T(8,128)(2,1)S(1)} %collective-permute-done.13), channel_id=1, source_target_pairs={{4,0},{8,4},{12,8},{16,12},{20,16},{24,20},{28,24},{32,28},{36,32}... | collective-permute-start | bytes 344072 | tf_op jit(solution)/shard_map/ppermute | solution.py:30
  116.0 23.8 %collective-permute-start.29 = (bf16[512,112]{0,1:T(8,128)(2,1)S(1)}, bf16[512,112]{0,1:T(8,128)(2,1)S(1)}, u32[]{:S(2)}, u32[]{:S(2)}) collective-permute-start(bf16[512,112]{0,1:T(8,128)(2,1)S(1)} %collective-permute-done.28), channel_id=1, source_target_pairs={{4,0},{8,4},{12,8},{16,12},{20,16},{24,20},{28,24},{32,28},{36,32}... | collective-permute-start | bytes 344072 | tf_op jit(solution)/shard_map/ppermute | solution.py:30
  117.9 7.9 %collective-permute-start.7 = (bf16[512,112]{0,1:T(8,128)(2,1)S(1)}, bf16[512,112]{0,1:T(8,128)(2,1)S(1)}, u32[]{:S(2)}, u32[]{:S(2)}) collective-permute-start(bf16[512,112]{0,1:T(8,128)(2,1)S(1)} %collective-permute-done.6), channel_id=1, source_target_pairs={{0,4},{4,8},{8,12},{12,16},{16,20},{20,24},{24,28},{28,32},{32,36}... | collective-permute-start | bytes 344072 | tf_op jit(solution)/shard_map/ppermute | solution.py:28
  163.8 8.4 %copy-start.13 = (f32[1024]{0:T(1024)S(1)}, f32[1024]{0:T(1024)}, u32[]{:S(2)}) copy-start(f32[1024]{0:T(1024)} %get-tuple-element.37) | copy-start | bytes 12292
  163.8 8.4 %copy-start.14 = (f32[1024]{0:T(1024)S(1)}, f32[1024]{0:T(1024)}, u32[]{:S(2)}) copy-start(f32[1024]{0:T(1024)} %get-tuple-element.38) | copy-start | bytes 12292
  167.0 5.2 %collective-permute-start.30 = (bf16[2,112]{0,1:T(8,128)(2,1)S(1)}, bf16[2,112]{0,1:T(8,128)(2,1)S(1)}, u32[]{:S(2)}, u32[]{:S(2)}) collective-permute-start(bf16[2,112]{0,1:T(8,128)(2,1)S(1)} %copy-done.9), channel_id=1, source_target_pairs={{0,64},{64,128},{128,192},{192,256},{256,320},{320,384},{384,448},... | collective-permute-start | bytes 1352 | tf_op jit(solution)/shard_map/ppermute | solution.py:40
  177.8 9.9 %collective-permute-start.37 = (bf16[4,2,112]{2,0,1:T(4,128)(2,1)S(1)}, bf16[4,2,112]{2,0,1:T(4,128)(2,1)S(1)}, u32[]{:S(2)}, u32[]{:S(2)}) collective-permute-start(bf16[4,2,112]{2,0,1:T(4,128)(2,1)S(1)} %get-tuple-element.55), channel_id=1, source_target_pairs={{0,64},{64,0},{128,192},{192,128},{256,320},{320,256},{384,448},{4... | collective-permute-start | bytes 5384 | tf_op jit(solution)/shard_map/ppermute | solution.py:49
  180.7 9.0 %collective-permute-start.34 = (bf16[4,1,273]{2,0,1:T(4,128)(2,1)S(1)}, bf16[4,1,273]{2,0,1:T(4,128)(2,1)S(1)}, u32[]{:S(2)}, u32[]{:S(2)}) collective-permute-start(bf16[4,1,273]{2,0,1:T(4,128)(2,1)S(1)} %convert_bitcast_fusion.3), channel_id=1, source_target_pairs={{0,64},{64,0},{128,192},{192,128},{256,320},{320,256},{384,448},{4... | collective-permute-start | bytes 6560 | tf_op jit(solution)/shard_map/ppermute | solution.py:49
  185.8 15.2 %collective-permute-start.31 = (bf16[1,4,273,112]{3,2,1,0:T(8,128)(2,1)S(1)}, bf16[1,4,273,112]{3,2,1,0:T(8,128)(2,1)S(1)}, u32[]{:S(2)}, u32[]{:S(2)}) collective-permute-start(bf16[1,4,273,112]{3,2,1,0:T(8,128)(2,1)S(1)} %convert_bitcast_fusion), channel_id=1, source_target_pairs={{0,64},{64,0},{128,192},{192,128},{256,320},{320,256},{384,448},{4... | collective-permute-start | bytes 733832 | tf_op jit(solution)/shard_map/ppermute | solution.py:49
  187.8 5.9 %collective-permute-start.38 = (bf16[4,2,112]{2,0,1:T(4,128)(2,1)S(1)}, bf16[4,2,112]{2,0,1:T(4,128)(2,1)S(1)}, u32[]{:S(2)}, u32[]{:S(2)}) collective-permute-start(bf16[4,2,112]{2,0,1:T(4,128)(2,1)S(1)} %fusion.88), channel_id=1, source_target_pairs={{0,128},{64,192},{128,0},{192,64},{256,384},{320,448},{384,256},{4... | collective-permute-start | bytes 5384 | tf_op jit(solution)/shard_map/ppermute | solution.py:49
  189.8 7.9 %collective-permute-start.35 = (bf16[4,1,273]{2,0,1:T(4,128)(2,1)S(1)}, bf16[4,1,273]{2,0,1:T(4,128)(2,1)S(1)}, u32[]{:S(2)}, u32[]{:S(2)}) collective-permute-start(bf16[4,1,273]{2,0,1:T(4,128)(2,1)S(1)} %fusion.89), channel_id=1, source_target_pairs={{0,128},{64,192},{128,0},{192,64},{256,384},{320,448},{384,256},{4... | collective-permute-start | bytes 6560 | tf_op jit(solution)/shard_map/ppermute | solution.py:49
  193.7 10.1 %collective-permute-start.39 = (bf16[4,2,112]{2,0,1:T(4,128)(2,1)S(1)}, bf16[4,2,112]{2,0,1:T(4,128)(2,1)S(1)}, u32[]{:S(2)}, u32[]{:S(2)}) collective-permute-start(bf16[4,2,112]{2,0,1:T(4,128)(2,1)S(1)} %fusion.90), channel_id=1, source_target_pairs={{0,256},{64,320},{128,384},{192,448},{256,0},{320,64},{384,128},{4... | collective-permute-start | bytes 5384 | tf_op jit(solution)/shard_map/ppermute | solution.py:49
  197.7 17.6 %collective-permute-start.36 = (bf16[4,1,273]{2,0,1:T(4,128)(2,1)S(1)}, bf16[4,1,273]{2,0,1:T(4,128)(2,1)S(1)}, u32[]{:S(2)}, u32[]{:S(2)}) collective-permute-start(bf16[4,1,273]{2,0,1:T(4,128)(2,1)S(1)} %fusion.87), channel_id=1, source_target_pairs={{0,256},{64,320},{128,384},{192,448},{256,0},{320,64},{384,128},{4... | collective-permute-start | bytes 6560 | tf_op jit(solution)/shard_map/ppermute | solution.py:49
  201.2 10.0 %collective-permute-start.32 = (bf16[1,4,273,112]{3,2,1,0:T(8,128)(2,1)S(1)}, bf16[1,4,273,112]{3,2,1,0:T(8,128)(2,1)S(1)}, u32[]{:S(2)}, u32[]{:S(2)}) collective-permute-start(bf16[1,4,273,112]{3,2,1,0:T(8,128)(2,1)S(1)} %fusion.72), channel_id=1, source_target_pairs={{0,128},{64,192},{128,0},{192,64},{256,384},{320,448},{384,256},{4... | collective-permute-start | bytes 733832 | tf_op jit(solution)/shard_map/ppermute | solution.py:49
  211.3 10.8 %collective-permute-start.33 = (bf16[1,4,273,112]{3,2,1,0:T(8,128)(2,1)S(1)}, bf16[1,4,273,112]{3,2,1,0:T(8,128)(2,1)S(1)}, u32[]{:S(2)}, u32[]{:S(2)}) collective-permute-start(bf16[1,4,273,112]{3,2,1,0:T(8,128)(2,1)S(1)} %fusion.51), channel_id=1, source_target_pairs={{0,256},{64,320},{128,384},{192,448},{256,0},{320,64},{384,128},{4... | collective-permute-start | bytes 733832 | tf_op jit(solution)/shard_map/ppermute | solution.py:49
  (16 other events, 71.6 us)
Sparse Core Ops, SparseCore 0:
  175.6 77.2 reduce-scatter.1
